TPU v7x, 128 devices: a whole 4x4x4 slice. The times are simulated.
128 devices in a mesh: blk: 32 (over y, x, core), grp: 4 (over z).
Axes of the slice: x: 4, y: 4, z: 4, core: 2. Of those that a mesh axis runs over, the one named last changes fastest.
Arguments:
- sky_map: bfloat16 [256, 1048576], P(None, ('blk', 'grp')), may hold values from -128 to 128
- fg_templates: bfloat16 [256, 16], replicated, may hold values from -0.375 to 0.375
- cycle_len: int32 [512], P(('blk', 'grp')), may hold values from 512 to 2048, as said below
- beam_profile: float32 [8, 1024], replicated, may hold values from 0.2 to 2
- beam_index: int32 [256], P('blk'), may hold values from 0 to 7
Outputs:
- filtered: float32 [1024, 256, 2, 1024], P(None, 'blk', None, 'grp')
Inputs may be any that keep to these rules, and one draw needn't show every extreme that they name: `cycle_len`: some cycle has exactly 2048 pixels.
All inputs are finite; a program needn't handle non-finite values.
Results may differ from a plain program's by a relative error of at most 0.0064.
Values may be sent and summed in bfloat16 or wider, within the bound.
No kernel may reach another device: no remote copies, remote signals or barrier semaphores. Data moves between devices by JAX's collectives and lax.ppermute only.
A program may use at most 192 MiB of HBM per device.

v0:
```python
import jax
import jax.numpy as jnp
from jax import lax
from jax.sharding import PartitionSpec as P

RPIX = 2048
L = 1024
M_DEV = 256


def cycle_table(length, m_width):
    slots = jnp.arange(RPIX, dtype=jnp.int32)
    orders = jnp.arange(m_width, dtype=jnp.int32)
    phase = orders[None, :] * (2 * slots[:, None] + 1) % (2 * length)
    angle = jnp.pi * phase.astype(jnp.float32) / length.astype(jnp.float32)
    weight = jnp.where(slots < length, 1.0, 0.0).astype(jnp.float32) * lax.rsqrt(
        length.astype(jnp.float32)
    )
    table = jnp.concatenate([jnp.cos(angle), -jnp.sin(angle)], axis=1) * weight[:, None]
    return table.astype(jnp.bfloat16)


def theta_table(cycle_ids, n_cycle):
    degrees = jnp.arange(L, dtype=jnp.int32)
    odd = 2 * cycle_ids + 1
    phase = degrees[:, None] * odd[None, :] % (4 * n_cycle)
    angle = jnp.pi * phase.astype(jnp.float32) / (2.0 * n_cycle)
    weight = jnp.sin(jnp.pi * odd.astype(jnp.float32) / (2.0 * n_cycle)) * (
        2.0 / jnp.sqrt(jnp.float32(n_cycle))
    )
    return (jnp.cos(angle) * weight[None, :]).astype(jnp.bfloat16)


def body(sky_map, fg_templates, cycle_len, beam_profile, beam_index):
    n_blk = lax.axis_size("blk")
    n_grp = lax.axis_size("grp")
    cycle_dev = cycle_len.shape[0]
    n_chan = sky_map.shape[0]
    chan_dev = n_chan // n_blk
    m_width = M_DEV * n_grp
    n_cycle = cycle_dev * n_blk * n_grp
    slots = jnp.arange(RPIX, dtype=jnp.int32)
    valid = (slots[None, :] < cycle_len[:, None]).reshape(-1)
    masked = jnp.where(valid[None, :], sky_map, jnp.zeros((), jnp.bfloat16))
    mode_amps = jnp.dot(fg_templates.T, masked, preferred_element_type=jnp.float32).astype(
        jnp.bfloat16
    )
    gram_part = jnp.dot(mode_amps, mode_amps.T, preferred_element_type=jnp.float32)
    cross_part = lax.dot_general(
        mode_amps, masked, (((1,), (1,)), ((), ())), preferred_element_type=jnp.float32
    )
    amps_wide = mode_amps.astype(jnp.float32)
    gram_sum = lax.psum(gram_part, ("blk", "grp"))
    lower = jnp.linalg.cholesky(gram_sum)
    basis = jax.scipy.linalg.solve_triangular(lower, amps_wide, lower=True)
    proj_part = jax.scipy.linalg.solve_triangular(lower, cross_part, lower=True)
    projected = lax.psum(proj_part, ("blk", "grp"))
    correction = jnp.dot(projected.T, basis, precision=lax.Precision.HIGHEST)
    cleaned = (masked.astype(jnp.float32) - correction).astype(jnp.bfloat16)
    pieces = []
    for local in range(cycle_dev):
        block = cleaned[:, local * RPIX : (local + 1) * RPIX]
        table = cycle_table(cycle_len[local], m_width)
        pieces.append(
            jnp.dot(block, table, preferred_element_type=jnp.float32).astype(jnp.bfloat16)
        )
    fourier = jnp.stack(pieces, 0).reshape(cycle_dev, n_chan, 2, m_width)
    position = jnp.arange(n_cycle, dtype=jnp.int32)
    moved = lax.all_to_all(
        lax.all_to_all(fourier, "blk", split_axis=1, concat_axis=0, tiled=True),
        "grp",
        split_axis=3,
        concat_axis=0,
        tiled=True,
    )
    group_id = position // (n_blk * cycle_dev)
    block_id = position // cycle_dev % n_blk
    cycle_ids = (block_id * n_grp + group_id) * cycle_dev + position % cycle_dev
    moved = moved.reshape(n_cycle, chan_dev * 2 * M_DEV)
    theta_tab = theta_table(cycle_ids, n_cycle)
    harmonic = jnp.dot(theta_tab, moved, preferred_element_type=jnp.float32).reshape(
        L, chan_dev, 2, M_DEV
    )
    onehot = (
        beam_index[:, None] == jnp.arange(beam_profile.shape[0], dtype=jnp.int32)[None, :]
    ).astype(jnp.float32)
    profiles = jnp.dot(onehot, beam_profile, precision=lax.Precision.HIGHEST)
    shaped = harmonic * profiles.T[:, :, None, None]
    orders = lax.axis_index("grp") * M_DEV + jnp.arange(M_DEV, dtype=jnp.int32)
    mweight = 0.25 + orders.astype(jnp.float32) / m_width
    weighted = shaped * mweight[None, None, None, :]
    power_part = jnp.sum(weighted * weighted, axis=(0, 2, 3))
    power = lax.psum(power_part, "grp")
    return weighted * lax.rsqrt(power / (2.0 * L * m_width) + 1e-06)[None, :, None, None]


def solution(mesh):
    return jax.shard_map(
        body,
        mesh=mesh,
        in_specs=(P(None, ("blk", "grp")), P(), P(("blk", "grp")), P(), P("blk")),
        out_specs=P(None, "blk", None, "grp"),
        check_vma=False,
    )
```

profile of v0, /device:TPU:0, one launch (start us, length us, event | category | flops | bytes accessed | tf_op | source)
XLA Modules:
  0.0 859.5 jit_solution(13465190245039165098)
XLA Ops:
  0.0 0.0 copy-start
  0.0 1.4 fusion.120
  6.2 0.7 fusion.87
  7.0 2.9 convolution_convert_fusion
  9.9 0.2 fusion.121
  10.1 3.4 fusion.50
  13.5 68.2 %psum.21 = f32[16,16]{0,1:T(8,128)S(1)} all-reduce(f32[16,16]{0,1:T(8,128)S(1)} %fusion.121), channel_id=1, replica_groups=mesh['blk'=32,'grp'=4] {'blk','grp'}, use_global_device_ids=true, to_apply=%region_0.1 | all-reduce | flops 256 | bytes 2048 | tf_op jit(solution)/shard_map/psum | solution.py:53
  81.7 0.1 copy.38
  81.8 1.5 cholesky.16
  83.3 0.7 compare_reduce_fusion
  84.0 0.7 fusion.88
  84.7 1.2 custom-call.10
  85.9 0.4 fusion.89
  86.3 0.2 fusion.91
  86.5 62.3 %psum.22 = f32[16,256]{1,0:T(8,128)S(1)} all-reduce(f32[16,256]{1,0:T(8,128)S(1)} %fusion.91), channel_id=1, replica_groups=mesh['blk'=32,'grp'=4] {'blk','grp'}, use_global_device_ids=true, to_apply=%region_3.4 | all-reduce | flops 4096 | bytes 32768 | tf_op jit(solution)/shard_map/psum | solution.py:57
  148.9 0.7 select_multiply_fusion.3
  149.6 8.9 %fusion.5 = bf16[256,8192]{1,0:T(8,128)(2,1)S(1)} fusion(f32[16,256]{1,0:T(8,128)S(1)} %psum.22, f32[16,8192]{1,0:T(8,128)S(1)} %fusion.89, bf16[256,8192]{1,0:T(8,128)(2,1)} %param.5, pred[8192]{0:T(1024)(128)(4,1)S(1)} %bitcast.62), kind=kOutput, calls=%fused_computation.16 | convolution fusion | flops 411041792 | bytes 8937472 | tf_op jit(solution)/shard_map/dot_general | solution.py:58
  158.5 0.0 copy-start.1
  158.5 451.2 %fusion.49 = (f32[2048,1024]{1,0:T(8,128)S(1)}, f32[2048,1024]{1,0:T(8,128)}, f32[2048,1024]{1,0:T(8,128)}, f32[2048,1024]{1,0:T(8,128)}, f32[2048,1024]{1,0:T(8...) fusion(f32[]{:T(128)S(6)} %convert_element_type.91, pred[]{:T(512)S(6)} %lt.110, ...), kind=kLoop, calls=%fused_computation.64 | loop fusion | flops 94371840 | bytes 67117088 | tf_op jit(solution)/shard_map/cos | solution.py:19
  609.7 0.0 copy-done.1
  609.7 6.3 fusion.51
  616.0 0.8 stack.15
  616.8 0.6 select_multiply_fusion.2
  617.4 8.5 fusion.54
  626.0 0.8 stack.16
  626.8 0.6 select_multiply_fusion.1
  627.4 9.5 %fusion.57 = bf16[256,2048]{1,0:T(8,128)(2,1)} fusion(f32[2048,1024]{1,0:T(8,128)} %get-tuple-element.7, f32[2048,1024]{1,0:T(8,128)} %get-tuple-element.10, f32[2048]{0:T(1024)S(1)} %select_multiply_fusion.1, bf16[256,8192]{1,0:T(8,128)(2,1)} %copy-done.1), kind=kOutput, calls=%fused_computation.72 | convolution fusion | flops 2160590848 | bytes 18882560 | tf_op jit(solution)/shard_map/dot_general | solution.py:65
  636.9 1.8 stack.17
  638.7 0.6 select_multiply_fusion
  639.3 9.5 %fusion.60 = bf16[256,2048]{1,0:T(8,128)(2,1)} fusion(f32[2048,1024]{1,0:T(8,128)} %get-tuple-element.8, f32[2048,1024]{1,0:T(8,128)} %get-tuple-element.9, f32[2048]{0:T(1024)S(1)} %select_multiply_fusion, bf16[256,8192]{1,0:T(8,128)(2,1)} %copy-done.1), kind=kOutput, calls=%fused_computation.73 | convolution fusion | flops 2160590848 | bytes 18882560 | tf_op jit(solution)/shard_map/dot_general | solution.py:65
  648.8 2.6 stack.18
  651.4 7.6 pad_maximum_fusion
  659.0 55.9 %all_to_all.33 = bf16[4,256,2,1024]{3,2,0,1:T(2,128)(2,1)S(1)} all-to-all(bf16[4,256,2,1024]{3,2,0,1:T(2,128)(2,1)S(1)} %pad_maximum_fusion), channel_id=1, replica_groups=mesh['blk'=32,'grp'=4] {'blk'}, dimensions={1} | all-to-all | bytes 8388608 | tf_op jit(solution)/shard_map/all_to_all | solution.py:70
  714.9 2.3 copy.55
  717.3 2.5 copy.44
  719.7 7.3 copy.45
  727.0 4.9 all-to-all-start.1
  731.9 0.1 sine_multiply_fusion
  732.0 0.0 copy-done
  732.0 0.2 convolution_bitcast_fusion
  732.2 49.1 %all-to-all-done.1 = bf16[128,8,2,1024]{0,1,2,3:T(8,128)(2,1)} async-done(((bf16[128,8,2,1024]{0,1,2,3:T(8,128)(2,1)}), bf16[128,8,2,1024]{0,1,2,3:T(8,128)(2,1)}, u32[]{:S(2)}, u32[]{:S(2)}) %all-to-all-start.1) | async-done | bytes 4194336 | tf_op jit(solution)/shard_map/all_to_all | solution.py:69
  781.3 9.0 %copy.47 = bf16[4,128,8,2,256]{4,3,2,1,0:T(2,128)(2,1)} copy(bf16[4,128,8,2,256]{1,2,3,4,0:T(8,128)(2,1)} %bitcast.18) | data formatting | bytes 8388608 | tf_op jit(solution)/shard_map/all_to_all | solution.py:69
  790.3 7.8 reshape.135
  798.1 6.5 copy.48
  804.6 17.2 %multiply_reduce_fusion = (f32[8]{0:T(128)S(1)}, f32[1024,8,2,256]{3,0,2,1:T(8,128)}) fusion(f32[256]{0:T(256)S(1)} %multiply_add_fusion.1, f32[1024,8]{0,1:T(8,128)S(1)} %convolution_bitcast_fusion, bf16[8,2,256,512]{3,2,1,0:T(8,128)(2,1)} %bitcast.55, f32[512]{0:T(512)S(1)} %sine_multiply_fusion, s32[512]{0:T(512)S(1)} %fusion.104), kind=kOutput, calls=%fused_computation.8 | convolution fusion | flops 4320133120 | bytes 21009440 | tf_op jit(solution)/shard_map/dot_general | solution.py:81
  821.9 8.8 %psum.23 = f32[8]{0:T(128)S(1)} all-reduce(f32[8]{0:T(128)S(1)} %get-tuple-element.17), channel_id=1, replica_groups=mesh['blk'=32,'grp'=4] {'grp'}, use_global_device_ids=true, to_apply=%region_5.6 | all-reduce | flops 8 | bytes 64 | tf_op jit(solution)/shard_map/psum | solution.py:93
  830.7 7.0 fusion.4
  837.8 21.5 %copy.49 = f32[1024,8,2,256]{3,2,1,0:T(2,128)} copy(f32[1024,8,2,256]{3,0,2,1:T(8,128)S(1)} %fusion.4) | data formatting | bytes 33554432 | tf_op jit(solution)/shard_map/mul | solution.py:94
  (9 shorter events, 0.1 us)
Async XLA Ops:
  0.0 732.0 %copy-start = (f32[8,1024]{1,0:T(8,128)S(1)}, f32[8,1024]{1,0:T(8,128)}, u32[]{:S(2)}) copy-start(f32[8,1024]{1,0:T(8,128)} %param.8) | copy-start | bytes 98308
  158.5 451.2 %copy-start.1 = (bf16[256,8192]{1,0:T(8,128)(2,1)}, bf16[256,8192]{1,0:T(8,128)(2,1)S(1)}, u32[]{:S(2)}) copy-start(bf16[256,8192]{1,0:T(8,128)(2,1)S(1)} %fusion.5) | copy-start | bytes 12582916
  719.7 12.3 %copy-start.2 = (s32[8]{0:T(128)S(1)}, s32[8]{0:T(128)}, u32[]{:S(2)}) copy-start(s32[8]{0:T(128)} %param.9) | copy-start | bytes 100
  727.0 54.3 %all-to-all-start.1 = ((bf16[128,8,2,1024]{0,1,2,3:T(8,128)(2,1)}), bf16[128,8,2,1024]{0,1,2,3:T(8,128)(2,1)}, u32[]{:S(2)}, u32[]{:S(2)}) async-start(bf16[128,8,2,1024]{0,1,2,3:T(8,128)(2,1)} %copy.45), calls=%async_computation.1 | async-start | bytes 8388608 | tf_op jit(solution)/shard_map/all_to_all | solution.py:69
where the time goes:
time: 867 us; the launch traced here: 859 us
  other arithmetic  473 us (55%)
  blocking collectives  195 us (22%)
  matrix products  67.2 us (8%)
  local copies, waits for them, and re-layouts  64.4 us (7%)
  waiting for transfers between devices  49.1 us (6%)
    cos x1, other arithmetic, cycle_table(): jnp.cos(angle)  451 us
    psum x1, blocking collectives, body(): gram_sum = lax.psum(gram_part, ('blk', 'grp'))  68.2 us
    psum x1, blocking collectives, body(): projected = lax.psum(proj_part, ('blk', 'grp'))  62.3 us
    all_to_all x1, blocking collectives, body(): lax.all_to_all(fourier, 'blk', split_axis=1, concat_axis=0, tiled=True)  55.9 us
    all_to_all x1, waiting for transfers between devices, body(): lax.all_to_all(lax.all_to_all(fourier, 'blk', split_axis=1, concat_axis=0...  49.1 us
    dot_general x4, matrix products, body(): jnp.dot(block, table, preferred_element_type=jnp.float32)  33.9 us
    mul x1, local copies, waits for them, and re-layouts, body(): weighted * lax.rsqrt(power / (2.0 * L * m_width) + 1e-06)[None, :, None,...  21.5 us
  transfers between devices with their start and end apart: 1, of which 1 were waited for; matrix products, arithmetic and copies ran while one was open for 0% of the time, Pallas kernels for 0%

commit v1 on v0

--- a/solution.py
+++ b/solution.py
@@ -2,6 +2,7 @@
 import jax.numpy as jnp
 from jax import lax
 from jax.sharding import PartitionSpec as P
+from jax.lax import all_gather
 
 RPIX = 2048
 L = 1024
@@ -54,7 +55,12 @@
     lower = jnp.linalg.cholesky(gram_sum)
     basis = jax.scipy.linalg.solve_triangular(lower, amps_wide, lower=True)
     proj_part = jax.scipy.linalg.solve_triangular(lower, cross_part, lower=True)
-    projected = lax.psum(proj_part, ("blk", "grp"))
+
+    def _draft_vector(s0):
+        mat_out = jnp.sum(all_gather(s0, ("blk", "grp")), axis=0)
+        return mat_out
+
+    projected = _draft_vector(proj_part)
     correction = jnp.dot(projected.T, basis, precision=lax.Precision.HIGHEST)
     cleaned = (masked.astype(jnp.float32) - correction).astype(jnp.bfloat16)
     pieces = []

time: 867 us -> 819 us (0.945)
  blocking collectives: 195 us -> 132 us
  between operations: 5.45 us -> 18.9 us
    psum x1 -> x0, blocking collectives: 62.3 us -> none  [body(): projected = lax.psum(proj_part, ('blk', 'grp'))]
  transfers between devices with their start and end apart: 1 -> 2, of which waited for: 1 -> 1; matrix products, arithmetic and copies ran while one was open for 0% -> 56% of each run, Pallas kernels for 0% -> 0%
where the time goes in v1:
time: 819 us; the launch traced here: 817 us
  other arithmetic  479 us (58%)
  blocking collectives  132 us (16%)
  matrix products  68.2 us (8%)
  local copies, waits for them, and re-layouts  65.6 us (8%)
  waiting for transfers between devices  49.2 us (6%)
  between operations  18.9 us (2%)
    cos x1, other arithmetic, cycle_table(): jnp.cos(angle)  455 us
    psum x1, blocking collectives, body(): gram_sum = lax.psum(gram_part, ('blk', 'grp'))  68.2 us
    all_to_all x1, blocking collectives, body(): lax.all_to_all(fourier, 'blk', split_axis=1, concat_axis=0, tiled=True)  55 us
    all_to_all x1, waiting for transfers between devices, body(): lax.all_to_all(lax.all_to_all(fourier, 'blk', split_axis=1, concat_axis=0...  49.1 us
    dot_general x4, matrix products, body(): jnp.dot(block, table, preferred_element_type=jnp.float32)  33.8 us
    mul x1, local copies, waits for them, and re-layouts, body(): weighted * lax.rsqrt(power / (2.0 * L * m_width) + 1e-06)[None, :, None,...  21.5 us
    dot_general x1, matrix products, body(): jnp.dot(theta_tab, moved, preferred_element_type=jnp.float32)  17.2 us
  transfers between devices with their start and end apart: 2, of which 1 were waited for; matrix products, arithmetic and copies ran while one was open for 56% of the time, Pallas kernels for 0%

profile of v1, /device:TPU:0, one launch (start us, length us, event | category | flops | bytes accessed | tf_op | source)
XLA Modules:
  0.0 817.3 jit_solution(11022977768885917442)
XLA Ops:
  6.5 0.0 all-gather.3.cloned.1.call-start
  6.5 0.8 fusion.87
  7.4 2.9 convolution_convert_fusion
  10.2 0.2 fusion.121
  10.5 3.4 fusion.50
  13.8 68.2 %psum.14 = f32[16,16]{0,1:T(8,128)S(1)} all-reduce(f32[16,16]{0,1:T(8,128)S(1)} %fusion.121), channel_id=1, replica_groups=mesh['blk'=32,'grp'=4] {'blk','grp'}, use_global_device_ids=true, to_apply=%region_0.1 | all-reduce | flops 256 | bytes 2048 | tf_op jit(solution)/shard_map/psum | solution.py:54
  82.1 0.1 copy.38
  82.1 1.5 cholesky.16
  83.6 0.6 compare_reduce_fusion
  84.3 0.6 fusion.88
  84.9 1.2 custom-call.10
  86.2 0.8 fusion.91
  87.0 0.0 all-gather.3.cloned.1.call-update
  87.0 0.7 fusion.120
  92.8 0.4 fusion.89
  93.3 0.7 select_multiply_fusion.3
  94.0 0.7 select_multiply_fusion.2
  94.7 0.6 select_multiply_fusion.1
  95.4 0.6 select_multiply_fusion
  96.0 454.7 %fusion.49 = (f32[2048,1024]{1,0:T(8,128)}, f32[2048,1024]{1,0:T(8,128)}, f32[2048,1024]{1,0:T(8,128)}, f32[2048,1024]{1,0:T(8,128)}, f32[2048,1024]{1,0:T(8,128...) fusion(f32[]{:T(128)S(6)} %convert_element_type.91, pred[]{:T(512)S(6)} %lt.110, ...), kind=kLoop, calls=%fused_computation.64 | loop fusion | flops 94371840 | bytes 67117088 | tf_op jit(solution)/shard_map/cos | solution.py:20
  550.7 0.0 all-gather.3.cloned.1.call-done
  550.7 1.8 reduce_sum.18
  552.5 9.2 %fusion.5 = bf16[256,8192]{1,0:T(8,128)(2,1)S(1)} fusion(f32[16,256]{1,0:T(8,128)S(1)} %reduce_sum.18, f32[16,8192]{1,0:T(8,128)S(1)} %fusion.89, bf16[256,8192]{1,0:T(8,128)(2,1)} %param.5, pred[8192]{0:T(1024)(128)(4,1)S(1)} %bitcast.64), kind=kOutput, calls=%fused_computation.16 | convolution fusion | flops 411041792 | bytes 8937472 | tf_op jit(solution)/shard_map/dot_general | solution.py:64
  561.7 1.9 copy-done.2
  563.6 6.3 fusion.51
  569.9 0.8 stack.15
  570.7 8.5 %fusion.54 = bf16[256,2048]{1,0:T(8,128)(2,1)S(1)} fusion(f32[2048,1024]{1,0:T(8,128)} %get-tuple-element.6, f32[2048,1024]{1,0:T(8,128)} %get-tuple-element.11, f32[2048]{0:T(1024)S(1)} %select_multiply_fusion.2, bf16[256,8192]{1,0:T(8,128)(2,1)} %copy-done.2), kind=kOutput, calls=%fused_computation.71 | convolution fusion | flops 2160590848 | bytes 18882560 | tf_op jit(solution)/shard_map/dot_general | solution.py:71
  579.2 0.8 stack.16
  580.0 9.5 %fusion.57 = bf16[256,2048]{1,0:T(8,128)(2,1)} fusion(f32[2048,1024]{1,0:T(8,128)} %get-tuple-element.7, f32[2048,1024]{1,0:T(8,128)} %get-tuple-element.10, f32[2048]{0:T(1024)S(1)} %select_multiply_fusion.1, bf16[256,8192]{1,0:T(8,128)(2,1)} %copy-done.2), kind=kOutput, calls=%fused_computation.72 | convolution fusion | flops 2160590848 | bytes 18882560 | tf_op jit(solution)/shard_map/dot_general | solution.py:71
  589.6 1.8 stack.17
  591.4 9.5 %fusion.60 = bf16[256,2048]{1,0:T(8,128)(2,1)} fusion(f32[2048,1024]{1,0:T(8,128)} %get-tuple-element.8, f32[2048,1024]{1,0:T(8,128)} %get-tuple-element.9, f32[2048]{0:T(1024)S(1)} %select_multiply_fusion, bf16[256,8192]{1,0:T(8,128)(2,1)} %copy-done.2), kind=kOutput, calls=%fused_computation.73 | convolution fusion | flops 2160590848 | bytes 18882560 | tf_op jit(solution)/shard_map/dot_general | solution.py:71
  600.9 2.6 stack.18
  603.5 7.6 pad_maximum_fusion
  611.1 55.0 %all_to_all.33 = bf16[4,256,2,1024]{3,2,0,1:T(2,128)(2,1)S(1)} all-to-all(bf16[4,256,2,1024]{3,2,0,1:T(2,128)(2,1)S(1)} %pad_maximum_fusion), channel_id=1, replica_groups=mesh['blk'=32,'grp'=4] {'blk'}, dimensions={1} | all-to-all | bytes 8388608 | tf_op jit(solution)/shard_map/all_to_all | solution.py:76
  666.1 2.3 copy.55
  668.4 2.5 copy.44
  670.9 7.3 copy.45
  678.2 4.9 all-to-all-start.1
  683.1 0.1 sine_multiply_fusion
  683.2 0.2 convolution_bitcast_fusion
  683.4 49.1 %all-to-all-done.1 = bf16[128,8,2,1024]{0,1,2,3:T(8,128)(2,1)} async-done(((bf16[128,8,2,1024]{0,1,2,3:T(8,128)(2,1)}), bf16[128,8,2,1024]{0,1,2,3:T(8,128)(2,1)}, u32[]{:S(2)}, u32[]{:S(2)}) %all-to-all-start.1) | async-done | bytes 4194336 | tf_op jit(solution)/shard_map/all_to_all | solution.py:75
  732.5 9.0 %copy.47 = bf16[4,128,8,2,256]{4,3,2,1,0:T(2,128)(2,1)} copy(bf16[4,128,8,2,256]{1,2,3,4,0:T(8,128)(2,1)} %bitcast.19) | data formatting | bytes 8388608 | tf_op jit(solution)/shard_map/all_to_all | solution.py:75
  741.5 7.8 reshape.135
  749.3 6.5 copy.48
  755.8 17.2 %multiply_reduce_fusion = (f32[8]{0:T(128)S(1)}, f32[1024,8,2,256]{3,0,2,1:T(8,128)}) fusion(f32[256]{0:T(256)S(1)} %multiply_add_fusion.1, f32[1024,8]{0,1:T(8,128)S(1)} %convolution_bitcast_fusion, bf16[8,2,256,512]{3,2,1,0:T(8,128)(2,1)} %bitcast.56, f32[512]{0:T(512)S(1)} %sine_multiply_fusion, s32[512]{0:T(512)S(1)} %fusion.104), kind=kOutput, calls=%fused_computation.8 | convolution fusion | flops 4320133120 | bytes 21009440 | tf_op jit(solution)/shard_map/dot_general | solution.py:87
  773.0 8.9 %psum.15 = f32[8]{0:T(128)S(1)} all-reduce(f32[8]{0:T(128)S(1)} %get-tuple-element.17), channel_id=1, replica_groups=mesh['blk'=32,'grp'=4] {'grp'}, use_global_device_ids=true, to_apply=%region_5.6 | all-reduce | flops 8 | bytes 64 | tf_op jit(solution)/shard_map/psum | solution.py:99
  781.9 7.0 fusion.4
  788.9 21.5 %copy.49 = f32[1024,8,2,256]{3,2,1,0:T(2,128)} copy(f32[1024,8,2,256]{3,0,2,1:T(8,128)S(1)} %fusion.4) | data formatting | bytes 33554432 | tf_op jit(solution)/shard_map/mul | solution.py:100
  (16 shorter events, 0.1 us)
Async XLA Ops:
  6.5 676.6 %copy-start = (f32[8,1024]{1,0:T(8,128)S(1)}, f32[8,1024]{1,0:T(8,128)}, u32[]{:S(2)}) copy-start(f32[8,1024]{1,0:T(8,128)} %param.8) | copy-start | bytes 98308
  6.5 80.5 %copy-start.3 = (s32[4]{0:T(128)S(1)}, s32[4]{0:T(128)}, u32[]{:S(2)}) copy-start(s32[4]{0:T(128)} %param.7) | copy-start | bytes 52
  6.5 544.2 %all-gather.3.cloned.1.call-start = ((), (), s32[]{:S(2)}) async-start(), calls=%async_computation.2 | async-start | bytes 2113536 | tf_op jit(solution)/shard_map/all_gather | solution.py:60
  552.5 11.1 %copy-start.1 = (f32[2048,1024]{1,0:T(8,128)S(1)}, f32[2048,1024]{1,0:T(8,128)}, u32[]{:S(2)}) copy-start(f32[2048,1024]{1,0:T(8,128)} %get-tuple-element.5) | copy-start | bytes 25165828
  561.7 1.9 copy-start.2
  670.9 12.3 %copy-start.4 = (s32[8]{0:T(128)S(1)}, s32[8]{0:T(128)}, u32[]{:S(2)}) copy-start(s32[8]{0:T(128)} %param.9) | copy-start | bytes 100
  678.2 54.3 %all-to-all-start.1 = ((bf16[128,8,2,1024]{0,1,2,3:T(8,128)(2,1)}), bf16[128,8,2,1024]{0,1,2,3:T(8,128)(2,1)}, u32[]{:S(2)}, u32[]{:S(2)}) async-start(bf16[128,8,2,1024]{0,1,2,3:T(8,128)(2,1)} %copy.45), calls=%async_computation.1 | async-start | bytes 8388608 | tf_op jit(solution)/shard_map/all_to_all | solution.py:75
Sparse Core Ops, SparseCore 0:
  87.1 61.5 all-gather.2
